TPU v7x, 256 devices: a whole 4x4x8 slice. The times are simulated.
256 devices in a mesh: dp: 32 (over x, z), mp: 8 (over y, core).
Axes of the slice: x: 4, y: 4, z: 8, core: 2. Of those that a mesh axis runs over, the one named last changes fastest.
Arguments:
- tokens: bfloat16 [8192, 8192], P(('dp', 'mp')), may hold values from -6 to 6
- upstream: bfloat16 [8192, 2, 28672], P(('dp', 'mp')), may hold values from -0.0625 to 0.0625
- deltas: bfloat16 [1024, 128, 128], P('mp'), may hold values from -0.5 to 0.5
- block_row: int32 [1024], P('mp'), may hold values from 0 to 63, as said below
- block_column: int32 [1024], P('mp'), may hold values from 0 to 55, as said below
- block_owner: int32 [1024], P('mp'), may hold values from 0 to 31, as said below
- block_count: int32 [8], P('mp'), may hold values from 64 to 128, as said below
Outputs:
- branch_out: bfloat16 [8192, 2, 28672], P('dp', None, 'mp')
- block_grads: float32 [8, 192, 128, 128], P('mp', 'dp')
Inputs may be any that keep to these rules, and one draw needn't show every extreme that they name: `block_row`: row tile of each slot's delta tile. `block_column`: column tile within the shard's gate columns (below 28) followed by its up columns; the tiles of one shard's slots are distinct. `block_owner`: among the live slots of one shard no dp index owns more than 6 tiles, and in every shard one dp index owns exactly 6. The live slots of a shard are its first block_count slots; some shard has all 128 live.
All inputs are finite; a program needn't handle non-finite values.
Results may differ from a plain program's by a relative error of at most 0.001.
Values may be sent and summed in bfloat16 or wider, within the bound.
No kernel may reach another device: no remote copies, remote signals or barrier semaphores. Data moves between devices by JAX's collectives and lax.ppermute only.
A program may use at most 128 MiB of HBM per device.

v0:
```python
import jax
import jax.numpy as jnp
from jax import lax
from jax.sharding import PartitionSpec as P


def pick_tiles(source, chosen):
    slot_ids = jnp.arange(chosen.shape[1], dtype=jnp.int32)
    source_index = jnp.sum(jnp.where(chosen, slot_ids[None, :], 0), axis=1)
    present = jnp.any(chosen, axis=1).astype(jnp.float32)
    return jnp.take(source, source_index, axis=0) * present[:, None, None]


def local(tokens, upstream, deltas, block_row, block_column, block_owner, block_count):
    model_width = tokens.shape[1]
    tile_size = deltas.shape[1]
    slot_count = deltas.shape[0]
    hidden = lax.all_to_all(upstream, "mp", split_axis=2, concat_axis=0, tiled=True)
    group_rows = hidden.shape[0]
    column_blocks = hidden.shape[1] * hidden.shape[2] // tile_size
    hidden_major = jnp.transpose(hidden.reshape(group_rows, column_blocks, tile_size), (1, 0, 2))
    upstream_chosen = jnp.take(hidden_major, block_column, axis=0)
    slot_ids = jnp.arange(slot_count, dtype=jnp.int32)
    live_slots = slot_ids < block_count[0]
    column_table = (
        live_slots[:, None]
        & (block_column[:, None] == jnp.arange(column_blocks, dtype=jnp.int32)[None, :])
    ).astype(jnp.float32)
    shard_rows = lax.all_gather(tokens, "mp", axis=0, tiled=True)
    row_count = shard_rows.shape[0]
    row_major = jnp.transpose(
        shard_rows.reshape(row_count, model_width // tile_size, tile_size), (1, 0, 2)
    )
    feature_tiles = jnp.take(row_major, block_row, axis=0)
    product = jnp.einsum("kni,kio->kno", feature_tiles, deltas, preferred_element_type=jnp.float32)
    rows_out = jnp.einsum("kc,kno->cno", column_table, product, precision=lax.Precision.HIGHEST)
    placed = rows_out
    grad_sum = jnp.einsum(
        "kni,kno->kio", feature_tiles, upstream_chosen, preferred_element_type=jnp.float32
    )
    placed, grad_sum = (placed, grad_sum)
    branch_out = jnp.transpose(placed.astype(jnp.bfloat16), (1, 0, 2)).reshape(
        group_rows, hidden.shape[1], hidden.shape[2]
    )
    dp_count = lax.axis_size("dp")
    owner_cap = 3 * slot_count // (2 * dp_count)
    owner_hot = (
        (block_owner[:, None] == jnp.arange(dp_count, dtype=jnp.int32)[None, :])
        & live_slots[:, None]
    ).astype(jnp.int32)
    before = jnp.cumsum(owner_hot, axis=0) - owner_hot
    owner_rank = jnp.sum(before * owner_hot, axis=1)
    summed = lax.psum(grad_sum, "dp")
    my_owner = lax.axis_index("dp")
    chosen = (
        live_slots[None, :]
        & (block_owner[None, :] == my_owner)
        & (owner_rank[None, :] == jnp.arange(owner_cap, dtype=jnp.int32)[:, None])
    )
    owned = pick_tiles(summed, chosen)
    return (branch_out, owned[None])


def solution(mesh):
    placed = (
        P(("dp", "mp"), None),
        P(("dp", "mp"), None, None),
        P("mp", None, None),
        P("mp"),
        P("mp"),
        P("mp"),
        P("mp"),
    )
    return jax.shard_map(
        local,
        mesh=mesh,
        in_specs=placed,
        out_specs=(P("dp", None, "mp"), P("mp", "dp", None, None)),
        check_vma=False,
    )
```

profile of v0, /device:TPU:1, one launch (start us, length us, event | category | flops | bytes accessed | tf_op | source)
XLA Modules:
  0.0 435.7 jit_solution(1149873122995598057)
XLA Ops:
  7.2 0.0 all-gather.2.cloned.1.call-start
  7.2 0.7 all-gather.2.cloned.1.call-update
  7.9 34.9 %copy.36 = bf16[32,2,28672]{0,1,2:T(2,128)(2,1)} copy(bf16[32,2,28672]{2,1,0:T(2,128)(2,1)} %param.8) | data formatting | bytes 7340032 | tf_op args[1]
  42.8 0.0 copy-start.2
  42.8 0.0 copy-start.1
  42.8 16.5 %reshape.95 = bf16[8,2,114688]{2,1,0:T(2,128)(2,1)} reshape(bf16[28672,2,32]{2,1,0:T(2,128)(2,1)} %bitcast.26) | data formatting | bytes 7340032
  59.4 7.6 %all-to-all-start = ((bf16[8,2,114688]{2,1,0:T(2,128)(2,1)}), bf16[8,2,114688]{2,1,0:T(2,128)(2,1)}, u32[]{:S(2)}, u32[]{:S(2)}) async-start(bf16[8,2,114688]{2,1,0:T(2,128)(2,1)} %reshape.95), calls=%async_computation | async-start | bytes 7340032 | tf_op jit(solution)/shard_map/all_to_all | solution.py:18
  66.9 0.0 all-reduce.2.cloned.1.call-start
  66.9 0.0 copy-done.2
  67.0 0.0 copy-done.1
  67.0 43.1 %all-to-all-done = bf16[8,2,114688]{2,1,0:T(2,128)(2,1)} async-done(((bf16[8,2,114688]{2,1,0:T(2,128)(2,1)}), bf16[8,2,114688]{2,1,0:T(2,128)(2,1)}, u32[]{:S(2)}, u32[]{:S(2)}) %all-to-all-start) | async-done | bytes 3670048 | tf_op jit(solution)/shard_map/all_to_all | solution.py:18
  110.1 11.6 %reshape.96 = bf16[28672,2,32]{2,1,0:T(2,128)(2,1)} reshape(bf16[8,2,114688]{2,1,0:T(2,128)(2,1)} %all-to-all-done) | data formatting | bytes 7340032
  121.7 35.0 %copy.37 = bf16[32,2,8,3584]{3,1,0,2:T(2,128)(2,1)} copy(bf16[32,2,8,3584]{0,1,3,2:T(2,128)(2,1)} %bitcast.25) | data formatting | bytes 7340032 | tf_op jit(solution)/shard_map/all_to_all | solution.py:18
  156.8 9.2 %reshape.67 = bf16[256,56,128]{2,1,0:T(8,128)(2,1)} reshape(bf16[8,32,2,3584]{3,2,1,0:T(2,128)(2,1)} %bitcast.30) | data formatting | bytes 7340032 | tf_op jit(solution)/shard_map/reshape | solution.py:21
  165.9 4.8 %copy.46 = bf16[256,56,128]{2,0,1:T(8,128)(2,1)} copy(bf16[256,56,128]{2,1,0:T(8,128)(2,1)} %reshape.67) | data formatting | bytes 7340032 | tf_op jit(solution)/shard_map/reshape | solution.py:21
  170.7 8.6 %gather_fusion.1 = bf16[128,256,128]{2,1,0:T(8,128)(2,1)} fusion(bf16[56,256,128]{2,1,0:T(8,128)(2,1)} %bitcast.27, s32[1024]{0:T(1024)S(1)} %pad_clamp_fusion.1), kind=kCustom, calls=%fused_computation.1 | custom fusion | bytes 16777728 | tf_op jit(solution)/shard_map/jit(_take)/gather | solution.py:22
  179.3 0.0 all-gather.2.cloned.1.call-done
  179.3 6.4 %copy.33 = bf16[256,8192]{0,1:T(8,128)(2,1)} copy(bf16[256,8192]{1,0:T(8,128)(2,1)} %all-gather.2.cloned.1.call-done) | data formatting | bytes 8388608 | tf_op jit(solution)/shard_map/all_gather | solution.py:29
  185.7 6.4 %copy.34 = bf16[256,64,128]{2,0,1:T(8,128)(2,1)} copy(bf16[256,64,128]{0,2,1:T(8,128)(2,1)} %bitcast.29) | data formatting | bytes 8388608 | tf_op jit(solution)/shard_map/reshape | solution.py:32
  192.1 8.7 %gather_fusion = bf16[128,256,128]{2,1,0:T(8,128)(2,1)} fusion(bf16[64,256,128]{2,1,0:T(8,128)(2,1)} %bitcast.28, s32[1024]{0:T(1024)S(1)} %pad_clamp_fusion.2), kind=kCustom, calls=%fused_computation | custom fusion | bytes 16777728 | tf_op jit(solution)/shard_map/jit(_take)/gather | solution.py:34
  200.8 11.9 %fusion.2 = f32[128,128,128]{2,1,0:T(8,128)} fusion(bf16[128,256,128]{2,1,0:T(8,128)(2,1)} %gather_fusion.1, pred[128]{0:T(512)(128)(4,1)S(1)} %get-tuple-element.4, bf16[128,256,128]{2,1,0:T(8,128)(2,1)} %gather_fusion, pred[128]{0:T(512)(128)(4,1)S(1)} %get-tuple-element.5), kind=kOutput, calls=%fused_computation.5 | convolution fusion | flops 1082130432 | bytes 25166080 | tf_op jit(solution)/shard_map/kni,kno->kio/dot_general | solution.py:38
  212.7 0.0 copy-start
  212.7 0.0 all-reduce.2.cloned.1.call-update
  213.4 0.0 copy-done
  213.4 0.1 fusion.11
  213.5 0.2 reduce_window_sum.11
  213.7 0.2 select_reduce_fusion
  213.9 0.1 fusion.18
  214.0 0.1 select_reduce_fusion.1
  214.2 13.5 %fusion.6 = f32[128,256,128]{2,1,0:T(8,128)} fusion(bf16[128,128,128]{2,1,0:T(8,128)(2,1)} %param.9, bf16[128,256,128]{2,1,0:T(8,128)(2,1)} %gather_fusion, pred[128]{0:T(512)(128)(4,1)S(1)} %get-tuple-element.5), kind=kOutput, calls=%fused_computation.12 | convolution fusion | flops 1077936128 | bytes 29360256 | tf_op jit(solution)/shard_map/kni,kio->kno/dot_general | solution.py:35
  227.7 22.6 %convert_bitcast_fusion = bf16[256,56,128]{2,1,0:T(8,128)(2,1)} fusion(f32[128,256,128]{2,1,0:T(8,128)} %fusion.6, s32[128]{0:T(128)S(1)} %copy-done.1, pred[128]{0:T(512)(128)(4,1)S(1)} %get-tuple-element.3), kind=kOutput, calls=%fused_computation.11 | convolution fusion | flops 2820421632 | bytes 20447872 | tf_op jit(solution)/shard_map/kc,kno->cno/dot_general | solution.py:36
  250.4 8.2 %reshape.66 = bf16[256,2,3584]{2,1,0:T(2,128)(2,1)} reshape(bf16[256,56,128]{2,1,0:T(8,128)(2,1)} %convert_bitcast_fusion) | data formatting | bytes 7340032 | tf_op jit(solution)/shard_map/reshape | solution.py:42
  258.5 165.6 %all-reduce.2.cloned.1.call-done = f32[128,128,128]{2,1,0:T(8,128)} async-done(((f32[128,128,128]{2,1,0:T(8,128)}), f32[128,128,128]{2,1,0:T(8,128)}) %all-reduce.2.cloned.1.call-update) | async-done | bytes 8388624 | tf_op jit(solution)/shard_map/psum | solution.py:53
  424.1 4.0 gather_fusion.2
  428.0 0.9 fusion.9
  (10 shorter events, 0.1 us)
Async XLA Ops:
  7.2 172.2 %all-gather.2.cloned.1.call-start = ((), (), s32[]{:S(2)}) async-start(), calls=%async_computation.1 | async-start | bytes 4718592 | tf_op jit(solution)/shard_map/all_gather | solution.py:29
  42.8 24.1 %copy-start.2 = (s32[128]{0:T(128)S(1)}, s32[128]{0:T(128)}, u32[]{:S(2)}) copy-start(s32[128]{0:T(128)} %param.10) | copy-start | bytes 1540
  42.8 24.1 %copy-start.1 = (s32[128]{0:T(128)S(1)}, s32[128]{0:T(128)}, u32[]{:S(2)}) copy-start(s32[128]{0:T(128)} %param.11) | copy-start | bytes 1540
  59.4 50.7 %all-to-all-start = ((bf16[8,2,114688]{2,1,0:T(2,128)(2,1)}), bf16[8,2,114688]{2,1,0:T(2,128)(2,1)}, u32[]{:S(2)}, u32[]{:S(2)}) async-start(bf16[8,2,114688]{2,1,0:T(2,128)(2,1)} %reshape.95), calls=%async_computation | async-start | bytes 7340032 | tf_op jit(solution)/shard_map/all_to_all | solution.py:18
  66.9 357.1 %all-reduce.2.cloned.1.call-start = ((), (), s32[]{:S(2)}) async-start(), calls=%async_computation.2 | async-start | bytes 16777216 | tf_op jit(solution)/shard_map/psum | solution.py:53
  212.7 0.7 copy-start
Sparse Core Ops, SparseCore 0:
  9.8 38.8 all-gather.1
  212.9 211.1 all-reduce.1
where the time goes:
time: 440 us; the launch traced here: 436 us
  waiting for transfers between devices  209 us (48%)
  local copies, waits for them, and re-layouts  154 us (35%)
  matrix products  48.1 us (11%)
  between operations  14.8 us (3%)
  starting transfers between devices  7.59 us (2%)
    psum x1, waiting for transfers between devices, local(): summed = lax.psum(grad_sum, 'dp')  166 us
    unnamed x9, local copies, waits for them, and re-layouts  63.1 us
    all_to_all x1, waiting for transfers between devices, local(): lax.all_to_all(upstream, 'mp', split_axis=2, concat_axis=0, tiled=True)  43.1 us
    all_to_all x1, local copies, waits for them, and re-layouts, local(): lax.all_to_all(upstream, 'mp', split_axis=2, concat_axis=0, tiled=True)  35 us
    dot_general x1, matrix products, local(): jnp.einsum('kc,kno->cno', column_table, product, precision=lax.Precision....  22.6 us
    reshape x2, local copies, waits for them, and re-layouts, local(): hidden.reshape(group_rows, column_blocks, tile_size)  14 us
    dot_general x1, matrix products, local(): jnp.einsum('kni,kio->kno', feature_tiles, deltas, preferred_element_type=...  13.5 us
    dot_general x1, matrix products, local(): jnp.einsum('kni,kno->kio', feature_tiles, upstream_chosen, preferred_elem...  11.9 us
  transfers between devices with their start and end apart: 3, of which 2 were waited for; matrix products, arithmetic and copies ran while one was open for 38% of the time, Pallas kernels for 0%

commit v1 on v0

--- a/solution.py
+++ b/solution.py
@@ -1,7 +1,24 @@
+import functools
 import jax
 import jax.numpy as jnp
 from jax import lax
 from jax.sharding import PartitionSpec as P
+
+
+def convert_the_plane(field, bus_axis):
+    nodes = lax.axis_size(bus_axis)
+    aux, u1 = (field, 0)
+    while 1 << u1 < nodes:
+        grid = []
+        for i0 in [*range(nodes)]:
+            grid.append((i0, i0 ^ 1 << u1))
+        later = lax.ppermute(aux, bus_axis, perm=grid)
+        aux = aux + later
+        u1 = u1 + 1
+    return aux
+
+
+use_weights_by_axis = functools.partial(convert_the_plane, bus_axis="dp")
 
 
 def pick_tiles(source, chosen):
@@ -50,7 +67,7 @@
     ).astype(jnp.int32)
     before = jnp.cumsum(owner_hot, axis=0) - owner_hot
     owner_rank = jnp.sum(before * owner_hot, axis=1)
-    summed = lax.psum(grad_sum, "dp")
+    summed = use_weights_by_axis(grad_sum)
     my_owner = lax.axis_index("dp")
     chosen = (
         live_slots[None, :]

time: 440 us -> 1570 us (3.57)
  waiting for transfers between devices: 209 us -> 1260 us
  other arithmetic: 1.61 us -> 60 us
    ppermute x0 -> x5, waiting for transfers between devices: none -> 1220 us  [convert_the_plane(): later = lax.ppermute(aux, bus_axis, perm=grid)]
    psum x1 -> x0, waiting for transfers between devices: 166 us -> none  [local(): summed = lax.psum(grad_sum, 'dp')]
    add x0 -> x5, other arithmetic: none -> 58.4 us  [convert_the_plane(): aux = aux + later]
  transfers between devices with their start and end apart: 3 -> 7, of which waited for: 2 -> 6; matrix products, arithmetic and copies ran while one was open for 38% -> 11% of each run, Pallas kernels for 0% -> 0%
where the time goes in v1:
time: 1570 us; the launch traced here: 1560 us
  waiting for transfers between devices  1260 us (80%)
  local copies, waits for them, and re-layouts  154 us (10%)
  other arithmetic  60 us (4%)
  matrix products  47.4 us (3%)
  starting transfers between devices  19.1 us (1%)
    ppermute x5, waiting for transfers between devices, convert_the_plane(): later = lax.ppermute(aux, bus_axis, perm=grid)  1220 us
    unnamed x9, local copies, waits for them, and re-layouts  63 us
    add x5, other arithmetic, convert_the_plane(): aux = aux + later  58.4 us
    all_to_all x1, waiting for transfers between devices, local(): lax.all_to_all(upstream, 'mp', split_axis=2, concat_axis=0, tiled=True)  43 us
    all_to_all x1, local copies, waits for them, and re-layouts, local(): lax.all_to_all(upstream, 'mp', split_axis=2, concat_axis=0, tiled=True)  35 us
  transfers between devices with their start and end apart: 7, of which 6 were waited for; matrix products, arithmetic and copies ran while one was open for 11% of the time, Pallas kernels for 0%

profile of v1, /device:TPU:1, one launch (start us, length us, event | category | flops | bytes accessed | tf_op | source)
XLA Modules:
  0.0 1556.4 jit_solution(786171603042988487)
XLA Ops:
  7.2 0.0 all-gather.2.cloned.1.call-start
  7.2 0.7 all-gather.2.cloned.1.call-update
  7.9 34.9 %copy.36 = bf16[32,2,28672]{0,1,2:T(2,128)(2,1)} copy(bf16[32,2,28672]{2,1,0:T(2,128)(2,1)} %param.8) | data formatting | bytes 7340032 | tf_op args[1]
  42.8 0.0 copy-start.2
  42.8 0.0 copy-start.1
  42.8 16.5 %reshape.95 = bf16[8,2,114688]{2,1,0:T(2,128)(2,1)} reshape(bf16[28672,2,32]{2,1,0:T(2,128)(2,1)} %bitcast.26) | data formatting | bytes 7340032
  59.4 8.1 all-to-all-start
  67.5 0.0 copy-done.2
  67.5 0.0 copy-done.1
  67.5 43.0 %all-to-all-done = bf16[8,2,114688]{2,1,0:T(2,128)(2,1)} async-done(((bf16[8,2,114688]{2,1,0:T(2,128)(2,1)}), bf16[8,2,114688]{2,1,0:T(2,128)(2,1)}, u32[]{:S(2)}, u32[]{:S(2)}) %all-to-all-start) | async-done | bytes 3670048 | tf_op jit(solution)/shard_map/all_to_all | solution.py:35
  110.6 11.6 reshape.96
  122.2 35.0 %copy.37 = bf16[32,2,8,3584]{3,1,0,2:T(2,128)(2,1)} copy(bf16[32,2,8,3584]{0,1,3,2:T(2,128)(2,1)} %bitcast.25) | data formatting | bytes 7340032 | tf_op jit(solution)/shard_map/all_to_all | solution.py:35
  157.2 9.2 reshape.67
  166.4 4.8 copy.46
  171.1 8.6 gather_fusion.1
  179.7 0.0 all-gather.2.cloned.1.call-done
  179.7 6.4 copy.33
  186.1 6.4 copy.34
  192.5 8.8 gather_fusion
  201.2 11.9 fusion.2
  213.2 0.2 collective-permute-start
  213.4 181.3 %collective-permute-done = f32[128,128,128]{2,1,0:T(8,128)} collective-permute-done((f32[128,128,128]{2,1,0:T(8,128)}, f32[128,128,128]{2,1,0:T(8,128)}, u32[]{:S(2)}, u32[]{:S(2)}) %collective-permute-start) | collective-permute-done | bytes 8388640 | tf_op jit(solution)/shard_map/ppermute | solution.py:15
  394.7 11.7 add.51
  406.4 1.6 collective-permute-start.1
  408.0 361.4 %collective-permute-done.1 = f32[128,128,128]{2,1,0:T(8,128)} collective-permute-done((f32[128,128,128]{2,1,0:T(8,128)}, f32[128,128,128]{2,1,0:T(8,128)}, u32[]{:S(2)}, u32[]{:S(2)}) %collective-permute-start.1) | collective-permute-done | bytes 8388640 | tf_op jit(solution)/shard_map/ppermute | solution.py:15
  769.4 11.7 add.52
  781.1 5.1 collective-permute-start.2
  786.2 361.4 %collective-permute-done.2 = f32[128,128,128]{2,1,0:T(8,128)} collective-permute-done((f32[128,128,128]{2,1,0:T(8,128)}, f32[128,128,128]{2,1,0:T(8,128)}, u32[]{:S(2)}, u32[]{:S(2)}) %collective-permute-start.2) | collective-permute-done | bytes 8388640 | tf_op jit(solution)/shard_map/ppermute | solution.py:15
  1147.6 11.7 add.53
  1159.3 0.0 copy-start
  1159.3 1.2 collective-permute-start.3
  1160.5 179.4 %collective-permute-done.3 = f32[128,128,128]{2,1,0:T(8,128)} collective-permute-done((f32[128,128,128]{2,1,0:T(8,128)}, f32[128,128,128]{2,1,0:T(8,128)}, u32[]{:S(2)}, u32[]{:S(2)}) %collective-permute-start.3) | collective-permute-done | bytes 8388640 | tf_op jit(solution)/shard_map/ppermute | solution.py:15
  1339.9 11.7 add.54
  1351.6 2.8 collective-permute-start.4
  1355.1 0.0 copy-done
  1355.1 0.1 fusion.11
  1355.2 0.2 reduce_window_sum.11
  1355.4 0.2 select_reduce_fusion
  1355.6 0.1 fusion.18
  1355.7 0.1 select_reduce_fusion.1
  1355.9 12.7 fusion.6
  1368.6 22.8 %convert_bitcast_fusion = bf16[256,56,128]{2,1,0:T(8,128)(2,1)} fusion(f32[128,256,128]{2,1,0:T(8,128)} %fusion.6, s32[128]{0:T(128)S(1)} %copy-done.1, pred[128]{0:T(512)(128)(4,1)S(1)} %get-tuple-element.3), kind=kOutput, calls=%fused_computation.11 | convolution fusion | flops 2820421632 | bytes 20447872 | tf_op jit(solution)/shard_map/kc,kno->cno/dot_general | solution.py:53
  1391.3 8.1 reshape.66
  1399.5 133.4 %collective-permute-done.4 = f32[128,128,128]{2,1,0:T(8,128)} collective-permute-done((f32[128,128,128]{2,1,0:T(8,128)}, f32[128,128,128]{2,1,0:T(8,128)}, u32[]{:S(2)}, u32[]{:S(2)}) %collective-permute-start.4) | collective-permute-done | bytes 8388640 | tf_op jit(solution)/shard_map/ppermute | solution.py:15
  1532.9 11.7 add.55
  1544.5 4.0 gather_fusion.2
  1548.5 0.9 fusion.9
  (10 shorter events, 0.1 us)
Async XLA Ops:
  7.2 172.6 %all-gather.2.cloned.1.call-start = ((), (), s32[]{:S(2)}) async-start(), calls=%async_computation.1 | async-start | bytes 4718592 | tf_op jit(solution)/shard_map/all_gather | solution.py:46
  42.8 24.7 %copy-start.2 = (s32[128]{0:T(128)S(1)}, s32[128]{0:T(128)}, u32[]{:S(2)}) copy-start(s32[128]{0:T(128)} %param.10) | copy-start | bytes 1540
  42.8 24.7 %copy-start.1 = (s32[128]{0:T(128)S(1)}, s32[128]{0:T(128)}, u32[]{:S(2)}) copy-start(s32[128]{0:T(128)} %param.11) | copy-start | bytes 1540
  59.4 51.2 %all-to-all-start = ((bf16[8,2,114688]{2,1,0:T(2,128)(2,1)}), bf16[8,2,114688]{2,1,0:T(2,128)(2,1)}, u32[]{:S(2)}, u32[]{:S(2)}) async-start(bf16[8,2,114688]{2,1,0:T(2,128)(2,1)} %reshape.95), calls=%async_computation | async-start | bytes 7340032 | tf_op jit(solution)/shard_map/all_to_all | solution.py:35
  213.2 181.5 %collective-permute-start = (f32[128,128,128]{2,1,0:T(8,128)}, f32[128,128,128]{2,1,0:T(8,128)}, u32[]{:S(2)}, u32[]{:S(2)}) collective-permute-start(f32[128,128,128]{2,1,0:T(8,128)} %fusion.2), channel_id=1, source_target_pairs={{0,8},{8,0},{16,24},{24,16},{32,40},{40,32},{48,56},{56,48},{64,72... | collective-permute-start | bytes 25165832 | tf_op jit(solution)/shard_map/ppermute | solution.py:15
  406.4 363.0 %collective-permute-start.1 = (f32[128,128,128]{2,1,0:T(8,128)}, f32[128,128,128]{2,1,0:T(8,128)}, u32[]{:S(2)}, u32[]{:S(2)}) collective-permute-start(f32[128,128,128]{2,1,0:T(8,128)} %add.51), channel_id=1, source_target_pairs={{0,16},{8,24},{16,0},{24,8},{32,48},{40,56},{48,32},{56,40},{64,80... | collective-permute-start | bytes 25165832 | tf_op jit(solution)/shard_map/ppermute | solution.py:15
  781.1 366.6 %collective-permute-start.2 = (f32[128,128,128]{2,1,0:T(8,128)}, f32[128,128,128]{2,1,0:T(8,128)}, u32[]{:S(2)}, u32[]{:S(2)}) collective-permute-start(f32[128,128,128]{2,1,0:T(8,128)} %add.52), channel_id=1, source_target_pairs={{0,32},{8,40},{16,48},{24,56},{32,0},{40,8},{48,16},{56,24},{64,96... | collective-permute-start | bytes 25165832 | tf_op jit(solution)/shard_map/ppermute | solution.py:15
  1159.3 195.8 %copy-start = (s32[128]{0:T(128)S(1)}, s32[128]{0:T(128)}, u32[]{:S(2)}) copy-start(s32[128]{0:T(128)} %param.12) | copy-start | bytes 1540
  1159.3 180.6 %collective-permute-start.3 = (f32[128,128,128]{2,1,0:T(8,128)}, f32[128,128,128]{2,1,0:T(8,128)}, u32[]{:S(2)}, u32[]{:S(2)}) collective-permute-start(f32[128,128,128]{2,1,0:T(8,128)} %add.53), channel_id=1, source_target_pairs={{0,64},{8,72},{16,80},{24,88},{32,96},{40,104},{48,112},{56,120},{... | collective-permute-start | bytes 25165832 | tf_op jit(solution)/shard_map/ppermute | solution.py:15
  1351.6 181.2 %collective-permute-start.4 = (f32[128,128,128]{2,1,0:T(8,128)}, f32[128,128,128]{2,1,0:T(8,128)}, u32[]{:S(2)}, u32[]{:S(2)}) collective-permute-start(f32[128,128,128]{2,1,0:T(8,128)} %add.54), channel_id=1, source_target_pairs={{0,128},{8,136},{16,144},{24,152},{32,160},{40,168},{48,176},{56,1... | collective-permute-start | bytes 25165832 | tf_op jit(solution)/shard_map/ppermute | solution.py:15
Sparse Core Ops, SparseCore 0:
  9.8 38.8 all-gather.1
